TPU v7x, 512 devices: a whole 4x4x16 slice. The times are simulated.
512 devices in a mesh: row: 32 (over z, core), col: 16 (over y, x).
Axes of the slice: x: 4, y: 4, z: 16, core: 2. Of those that a mesh axis runs over, the one named last changes fastest.
Arguments:
- pressure_in: float32 [1024, 256, 128], P('row', 'col'), may hold values from -6 to 6
- source: float32 [1024, 256, 128], P('row', 'col'), may hold values from -18 to 18
- permeability: float32 [1024, 256, 128], P('row', 'col'), may hold values from 0.2 to 5
Outputs:
- pressure_out: float32 [1024, 256, 128], P('row', 'col')
All inputs are finite; a program needn't handle non-finite values.
Results may differ from a plain program's by a relative error of at most 0.0001.
Values sent between devices are 32-bit elements; how exact they have to be, the bound alone decides.
No kernel may reach another device: no remote copies, remote signals or barrier semaphores. Data moves between devices by JAX's collectives and lax.ppermute only.
A program may use at most 128 MiB of HBM per device.

v0:
```python
import jax
import jax.numpy as jnp
from jax import lax
from jax.sharding import PartitionSpec as P

LEVELS = 3
NU1 = 2
NU2 = 2
CSWEEPS = 16
OMEGA = 0.8


def padded_2(array, sides, width):
    for axis, dim in sides:
        size, length = (lax.axis_size(axis), array.shape[dim])
        up = [(i, (i + 1) % size) for i in range(size)]
        down = [(j, i) for i, j in up]
        last = lax.slice_in_dim(array, length - width, length, axis=dim)
        first = lax.slice_in_dim(array, 0, width, axis=dim)
        before = lax.ppermute(last, axis, up)
        after = lax.ppermute(first, axis, down)
        array = jnp.concatenate([before, array, after], axis=dim)
    return array


def harmonic(left, right, scale):
    return 2.0 * left * right / (left + right) * scale


def coefficients(padded, center, scale):
    west_x = harmonic(padded[:-2, 1:-1], center, scale)
    east_x = harmonic(center, padded[2:, 1:-1], scale)
    west_y = harmonic(padded[1:-1, :-2], center, scale)
    east_y = harmonic(center, padded[1:-1, 2:], scale)
    inner = harmonic(center[:, :, :-1], center[:, :, 1:], scale)
    below = jnp.concatenate([2.0 * center[:, :, :1] * scale, inner], axis=2)
    above = jnp.concatenate([inner, 2.0 * center[:, :, -1:] * scale], axis=2)
    diagonal = west_x + east_x + west_y + east_y + below + above
    return (west_x, east_x, west_y, east_y, below, above, diagonal)


def apply_operator(padded, center, faces):
    west_x, east_x, west_y, east_y, below, above, diagonal = faces
    zero_plane = jnp.zeros_like(center[:, :, :1])
    under = jnp.concatenate([zero_plane, center[:, :, :-1]], axis=2)
    over = jnp.concatenate([center[:, :, 1:], zero_plane], axis=2)
    beside_all = west_x * padded[:-2, 1:-1] + east_x * padded[2:, 1:-1]
    beside_all = beside_all + west_y * padded[1:-1, :-2] + east_y * padded[1:-1, 2:]
    beside_all = beside_all + below * under + above * over
    return diagonal * center - beside_all


def jacobi_sweep(pressure, right_side, faces, padder):
    return (
        pressure
        + OMEGA * (right_side - apply_operator(padder(pressure), pressure, faces)) / faces[6]
    )


def first_sweep(right_side, faces):
    return OMEGA * right_side / faces[6]


def coarsen(field):
    size_x, size_y, size_z = field.shape
    return field.reshape(size_x // 2, 2, size_y // 2, 2, size_z // 2, 2).mean(axis=(1, 3, 5))


def prolong(field):
    return jnp.repeat(jnp.repeat(jnp.repeat(field, 2, axis=0), 2, axis=1), 2, axis=2)


def mesh_pad(field):
    return padded_2(field, (("row", 0), ("col", 1)), 1)


def perm_pad(field):
    return padded_2(field, (("row", 0), ("col", 1)), 1)


def band_pad(field):
    extended = padded_2(field, (("row", 0),), 1)
    return jnp.pad(extended, ((0, 0), (1, 1), (0, 0)), mode="wrap")


def band_perm_pad(field):
    extended = padded_2(field, (("row", 0),), 1)
    return jnp.pad(extended, ((0, 0), (1, 1), (0, 0)), mode="wrap")


def coarse_solve(right_side, faces, padder):
    start = first_sweep(right_side, faces)

    def one_sweep(sweep_index, current):
        return jacobi_sweep(current, right_side, faces, padder)

    return lax.fori_loop(1, CSWEEPS, one_sweep, start)


def on_device(pressure_in, source, permeability):
    perms = [permeability]
    for depth_level in range(LEVELS):
        perms.append(coarsen(perms[depth_level]))
    pressure = pressure_in
    right_side = source
    states = []
    all_faces = [
        coefficients(perm_pad(perms[depth_level]), perms[depth_level], 0.25**depth_level)
        for depth_level in range(LEVELS)
    ]
    for depth_level in range(LEVELS):
        faces = all_faces[depth_level]
        if depth_level == 0:
            for sweep_index in range(NU1):
                pressure = jacobi_sweep(pressure, right_side, faces, mesh_pad)
        else:
            pressure = first_sweep(right_side, faces)
            pressure = jacobi_sweep(pressure, right_side, faces, mesh_pad)
        states.append((pressure, right_side))
        residual = right_side - apply_operator(mesh_pad(pressure), pressure, faces)
        right_side = coarsen(residual)
    coarse_perm = perms[LEVELS]
    size_x, size_y, size_z = right_side.shape
    coarse_scale = 0.25**LEVELS
    band_rhs, band_perm = (
        lax.all_gather(right_side, "col", axis=1, tiled=True),
        lax.all_gather(coarse_perm, "col", axis=1, tiled=True),
    )
    band_faces = coefficients(band_perm_pad(band_perm), band_perm, coarse_scale)
    solved = coarse_solve(band_rhs, band_faces, band_pad)
    correction = lax.dynamic_slice_in_dim(solved, lax.axis_index("col") * size_y, size_y, 1)
    for depth_level in range(LEVELS - 1, -1, -1):
        pressure, right_side = states[depth_level]
        pressure = pressure + prolong(correction)
        for sweep_index in range(NU2):
            pressure = jacobi_sweep(pressure, right_side, all_faces[depth_level], mesh_pad)
        correction = pressure
    return correction


def solution(mesh):
    placed = (P("row", "col", None), P("row", "col", None), P("row", "col", None))
    return jax.shard_map(
        on_device, mesh=mesh, in_specs=placed, out_specs=P("row", "col", None), check_vma=False
    )
```

profile of v0, /device:TPU:30, one launch (start us, length us, event | category | flops | bytes accessed | tf_op | source)
XLA Modules:
  0.0 433.4 jit_solution(4026333652085899989)
XLA Ops:
  0.7 8.9 %collective-permute-start.3 = (f32[1,16,128]{2,1,0:T(8,128)S(1)}, f32[1,16,128]{2,1,0:T(8,128)S(1)}, u32[]{:S(2)}, u32[]{:S(2)}) collective-permute-start(f32[1,16,128]{2,1,0:T(8,128)S(1)} %get-tuple-element.177), channel_id=1, source_target_pairs={{16,0},{32,16},{48,32},{64,48},{80,64},{96,80},{112,96},{128,112},... | collective-permute-start | bytes 24584 | tf_op jit(solution)/shard_map/ppermute | solution.py:21
  17.4 18.9 %reshape.48 = f32[16,2,8,2,64,2]{5,4,3,2,1,0:T(8,128)} reshape(f32[32,16,128]{2,1,0:T(8,128)} %param.7) | data formatting | bytes 524288 | tf_op jit(solution)/shard_map/reshape | solution.py:66
  36.4 7.0 %reduce_sum.55 = f32[16,8,64]{2,1,0:T(8,128)S(1)} reduce(f32[16,2,8,2,64,2]{5,4,3,2,1,0:T(8,128)} %reshape.48, f32[]{:T(128)} %constant.23.clone.1), dimensions={1,3,5}, to_apply=%region_1.0 | reduce | flops 57344 | bytes 294916 | tf_op jit(solution)/shard_map/reduce_sum | solution.py:66
  48.9 21.4 %all_gather.7 = f32[4,32,16]{2,0,1:T(4,128)S(1)} all-gather(f32[4,2,16]{2,0,1:T(4,128)S(1)} %broadcast_multiply_fusion.2), channel_id=1, replica_groups=mesh['row'=32,'col'=16] {'col'}, dimensions={1}, use_global_device_ids=true | all-gather | bytes 8704 | tf_op jit(solution)/shard_map/all_gather | solution.py:127
  71.7 4.7 %collective-permute-start.4 = (f32[34,1,128]{2,1,0:T(1,128)S(1)}, f32[34,1,128]{2,1,0:T(1,128)S(1)}, u32[]{:S(2)}, u32[]{:S(2)}) collective-permute-start(f32[34,1,128]{2,1,0:T(1,128)S(1)} %get-tuple-element.156), channel_id=1, source_target_pairs={{0,1},{1,2},{2,3},{3,4},{4,5},{5,6},{6,7},{7,8},{8,9},{9,10},{10,1... | collective-permute-start | bytes 52232 | tf_op jit(solution)/shard_map/ppermute | solution.py:20
  78.4 7.2 %collective-permute-start.8 = (f32[34,1,128]{2,1,0:T(1,128)S(1)}, f32[34,1,128]{2,1,0:T(1,128)S(1)}, u32[]{:S(2)}, u32[]{:S(2)}) collective-permute-start(f32[34,1,128]{2,1,0:T(1,128)S(1)} %get-tuple-element.157), channel_id=1, source_target_pairs={{0,1},{1,2},{2,3},{3,4},{4,5},{5,6},{6,7},{7,8},{8,9},{9,10},{10,1... | collective-permute-start | bytes 52232 | tf_op jit(solution)/shard_map/ppermute | solution.py:20
  90.6 4.0 collective-permute-done.9
  124.7 6.6 %collective-permute-start.20 = (f32[18,1,64]{2,1,0:T(1,128)S(1)}, f32[18,1,64]{2,1,0:T(1,128)S(1)}, u32[]{:S(2)}, u32[]{:S(2)}) collective-permute-start(f32[18,1,64]{2,1,0:T(1,128)S(1)} %get-tuple-element.192), channel_id=1, source_target_pairs={{0,1},{1,2},{2,3},{3,4},{4,5},{5,6},{6,7},{7,8},{8,9},{9,10},{10,1... | collective-permute-start | bytes 13832 | tf_op jit(solution)/shard_map/ppermute | solution.py:20
  134.4 18.1 %reshape.47 = f32[16,2,8,2,64,2]{5,4,3,2,1,0:T(8,128)} reshape(f32[32,16,128]{2,1,0:T(8,128)S(1)} %fusion.47) | data formatting | bytes 524288 | tf_op jit(solution)/shard_map/reshape | solution.py:66
  152.5 7.0 %reduce_sum.54 = f32[16,8,64]{2,1,0:T(8,128)S(1)} reduce(f32[16,2,8,2,64,2]{5,4,3,2,1,0:T(8,128)} %reshape.47, f32[]{:T(128)} %constant.23.clone.1), dimensions={1,3,5}, to_apply=%region_0.0 | reduce | flops 57344 | bytes 294916 | tf_op jit(solution)/shard_map/reduce_sum | solution.py:66
  164.1 7.2 %collective-permute-start.24 = (f32[18,1,64]{2,1,0:T(1,128)S(1)}, f32[18,1,64]{2,1,0:T(1,128)S(1)}, u32[]{:S(2)}, u32[]{:S(2)}) collective-permute-start(f32[18,1,64]{2,1,0:T(1,128)S(1)} %get-tuple-element.189), channel_id=1, source_target_pairs={{0,1},{1,2},{2,3},{3,4},{4,5},{5,6},{6,7},{7,8},{8,9},{9,10},{10,1... | collective-permute-start | bytes 13832 | tf_op jit(solution)/shard_map/ppermute | solution.py:20
  176.3 3.9 collective-permute-done.25
  184.7 3.3 collective-permute-start.28
  190.6 6.7 %collective-permute-start.32 = (f32[10,1,32]{2,1,0:T(1,128)}, f32[10,1,32]{2,1,0:T(1,128)}, u32[]{:S(2)}, u32[]{:S(2)}) collective-permute-start(f32[10,1,32]{2,1,0:T(1,128)} %get-tuple-element.228), channel_id=1, source_target_pairs={{0,1},{1,2},{2,3},{3,4},{4,5},{5,6},{6,7},{7,8},{8,9},{9,10},{10,1... | collective-permute-start | bytes 3848 | tf_op jit(solution)/shard_map/ppermute | solution.py:20
  211.7 4.9 %collective-permute-start.36 = (f32[10,1,32]{2,1,0:T(1,128)S(1)}, f32[10,1,32]{2,1,0:T(1,128)S(1)}, u32[]{:S(2)}, u32[]{:S(2)}) collective-permute-start(f32[10,1,32]{2,1,0:T(1,128)S(1)} %get-tuple-element.225), channel_id=1, source_target_pairs={{0,1},{1,2},{2,3},{3,4},{4,5},{5,6},{6,7},{7,8},{8,9},{9,10},{10,1... | collective-permute-start | bytes 3848 | tf_op jit(solution)/shard_map/ppermute | solution.py:20
  218.6 6.8 %collective-permute-done.37 = f32[10,1,32]{2,1,0:T(1,128)S(1)} collective-permute-done((f32[10,1,32]{2,1,0:T(1,128)S(1)}, f32[10,1,32]{2,1,0:T(1,128)S(1)}, u32[]{:S(2)}, u32[]{:S(2)}) %collective-permute-start.37) | collective-permute-done | bytes 1312 | tf_op jit(solution)/shard_map/ppermute | solution.py:21
  232.5 3.9 collective-permute-start.41
  236.5 4.8 %collective-permute-done.41 = f32[10,1,32]{2,1,0:T(1,128)S(1)} collective-permute-done((f32[10,1,32]{2,1,0:T(1,128)S(1)}, f32[10,1,32]{2,1,0:T(1,128)S(1)}, u32[]{:S(2)}, u32[]{:S(2)}) %collective-permute-start.41) | collective-permute-done | bytes 1312 | tf_op jit(solution)/shard_map/ppermute | solution.py:21
  242.4 20.3 %all_gather.6 = f32[4,32,16]{2,0,1:T(4,128)S(1)} all-gather(f32[4,2,16]{2,0,1:T(4,128)S(1)} %broadcast_multiply_fusion.3), channel_id=1, replica_groups=mesh['row'=32,'col'=16] {'col'}, dimensions={1}, use_global_device_ids=true | all-gather | bytes 8704 | tf_op jit(solution)/shard_map/all_gather | solution.py:126
  263.9 68.6 %while.10 = (s32[]{:T(128)}, f32[4,32,16]{1,2,0:T(8,128)S(1)}, f32[4,32,16]{1,2,0:T(8,128)S(1)}, f32[4,32,16]{1,2,0:T(8,128)S(1)}, f32[4,32,16]{1,2,0:T(8,128)S(...) while((s32[]{:T(128)}, f32[4,32,16]{1,2,0:T(8,128)S(1)}, ...), condition=%wide.region_7.8_spmd, body=%wide.region_6.7_spmd.sunk | while | flops 43010 | bytes 279997 | solution.py:97
  337.2 4.9 %collective-permute-start.46 = (f32[10,1,32]{2,1,0:T(1,128)S(1)}, f32[10,1,32]{2,1,0:T(1,128)S(1)}, u32[]{:S(2)}, u32[]{:S(2)}) collective-permute-start(f32[10,1,32]{2,1,0:T(1,128)S(1)} %get-tuple-element.221), channel_id=1, source_target_pairs={{0,1},{1,2},{2,3},{3,4},{4,5},{5,6},{6,7},{7,8},{8,9},{9,10},{10,1... | collective-permute-start | bytes 3848 | tf_op jit(solution)/shard_map/ppermute | solution.py:20
  344.1 6.8 %collective-permute-done.47 = f32[10,1,32]{2,1,0:T(1,128)S(1)} collective-permute-done((f32[10,1,32]{2,1,0:T(1,128)S(1)}, f32[10,1,32]{2,1,0:T(1,128)S(1)}, u32[]{:S(2)}, u32[]{:S(2)}) %collective-permute-start.47) | collective-permute-done | bytes 1312 | tf_op jit(solution)/shard_map/ppermute | solution.py:21
  357.9 3.9 collective-permute-start.51
  362.0 4.8 %collective-permute-done.51 = f32[10,1,32]{2,1,0:T(1,128)S(1)} collective-permute-done((f32[10,1,32]{2,1,0:T(1,128)S(1)}, f32[10,1,32]{2,1,0:T(1,128)S(1)}, u32[]{:S(2)}, u32[]{:S(2)}) %collective-permute-start.51) | collective-permute-done | bytes 1312 | tf_op jit(solution)/shard_map/ppermute | solution.py:21
  374.2 3.9 collective-permute-start.55
  378.2 4.9 %collective-permute-done.55 = f32[18,1,64]{2,1,0:T(1,128)S(1)} collective-permute-done((f32[18,1,64]{2,1,0:T(1,128)S(1)}, f32[18,1,64]{2,1,0:T(1,128)S(1)}, u32[]{:S(2)}, u32[]{:S(2)}) %collective-permute-start.55) | collective-permute-done | bytes 4640 | tf_op jit(solution)/shard_map/ppermute | solution.py:21
  390.5 3.9 collective-permute-start.59
  394.5 4.9 %collective-permute-done.59 = f32[18,1,64]{2,1,0:T(1,128)S(1)} collective-permute-done((f32[18,1,64]{2,1,0:T(1,128)S(1)}, f32[18,1,64]{2,1,0:T(1,128)S(1)}, u32[]{:S(2)}, u32[]{:S(2)}) %collective-permute-start.59) | collective-permute-done | bytes 4640 | tf_op jit(solution)/shard_map/ppermute | solution.py:21
  407.7 3.9 collective-permute-start.63
  411.8 4.9 %collective-permute-done.63 = f32[34,1,128]{2,1,0:T(1,128)S(1)} collective-permute-done((f32[34,1,128]{2,1,0:T(1,128)S(1)}, f32[34,1,128]{2,1,0:T(1,128)S(1)}, u32[]{:S(2)}, u32[]{:S(2)}) %collective-permute-start.63) | collective-permute-done | bytes 17440 | tf_op jit(solution)/shard_map/ppermute | solution.py:21
  423.4 3.9 collective-permute-start.67
  427.5 4.9 %collective-permute-done.67 = f32[34,1,128]{2,1,0:T(1,128)S(1)} collective-permute-done((f32[34,1,128]{2,1,0:T(1,128)S(1)}, f32[34,1,128]{2,1,0:T(1,128)S(1)}, u32[]{:S(2)}, u32[]{:S(2)}) %collective-permute-start.67) | collective-permute-done | bytes 17440 | tf_op jit(solution)/shard_map/ppermute | solution.py:21
  (457 shorter events, 209.8 us)
Async XLA Ops:
  0.7 70.9 %collective-permute-start.2 = (f32[1,16,128]{2,1,0:T(8,128)S(1)}, f32[1,16,128]{2,1,0:T(8,128)S(1)}, u32[]{:S(2)}, u32[]{:S(2)}) collective-permute-start(f32[1,16,128]{2,1,0:T(8,128)S(1)} %get-tuple-element.178), channel_id=1, source_target_pairs={{0,16},{16,32},{32,48},{48,64},{64,80},{80,96},{96,112},{112,128},... | collective-permute-start | bytes 24584 | tf_op jit(solution)/shard_map/ppermute | solution.py:20
  0.7 70.9 %collective-permute-start.3 = (f32[1,16,128]{2,1,0:T(8,128)S(1)}, f32[1,16,128]{2,1,0:T(8,128)S(1)}, u32[]{:S(2)}, u32[]{:S(2)}) collective-permute-start(f32[1,16,128]{2,1,0:T(8,128)S(1)} %get-tuple-element.177), channel_id=1, source_target_pairs={{16,0},{32,16},{48,32},{64,48},{80,64},{96,80},{112,96},{128,112},... | collective-permute-start | bytes 24584 | tf_op jit(solution)/shard_map/ppermute | solution.py:21
  10.4 67.9 %collective-permute-start.6 = (f32[1,16,128]{2,1,0:T(8,128)S(1)}, f32[1,16,128]{2,1,0:T(8,128)S(1)}, u32[]{:S(2)}, u32[]{:S(2)}) collective-permute-start(f32[1,16,128]{2,1,0:T(8,128)S(1)} %get-tuple-element.182), channel_id=1, source_target_pairs={{0,16},{16,32},{32,48},{48,64},{64,80},{80,96},{96,112},{112,128},... | collective-permute-start | bytes 24584 | tf_op jit(solution)/shard_map/ppermute | solution.py:20
  10.4 68.0 %collective-permute-start.7 = (f32[1,16,128]{2,1,0:T(8,128)S(1)}, f32[1,16,128]{2,1,0:T(8,128)S(1)}, u32[]{:S(2)}, u32[]{:S(2)}) collective-permute-start(f32[1,16,128]{2,1,0:T(8,128)S(1)} %get-tuple-element.181), channel_id=1, source_target_pairs={{16,0},{32,16},{48,32},{64,48},{80,64},{96,80},{112,96},{128,112},... | collective-permute-start | bytes 24584 | tf_op jit(solution)/shard_map/ppermute | solution.py:21
  71.7 16.0 %collective-permute-start.4 = (f32[34,1,128]{2,1,0:T(1,128)S(1)}, f32[34,1,128]{2,1,0:T(1,128)S(1)}, u32[]{:S(2)}, u32[]{:S(2)}) collective-permute-start(f32[34,1,128]{2,1,0:T(1,128)S(1)} %get-tuple-element.156), channel_id=1, source_target_pairs={{0,1},{1,2},{2,3},{3,4},{4,5},{5,6},{6,7},{7,8},{8,9},{9,10},{10,1... | collective-permute-start | bytes 52232 | tf_op jit(solution)/shard_map/ppermute | solution.py:20
  76.4 14.2 %collective-permute-start.5 = (f32[34,1,128]{2,1,0:T(1,128)S(1)}, f32[34,1,128]{2,1,0:T(1,128)S(1)}, u32[]{:S(2)}, u32[]{:S(2)}) collective-permute-start(f32[34,1,128]{2,1,0:T(1,128)S(1)} %get-tuple-element.155), channel_id=1, source_target_pairs={{1,0},{2,1},{3,2},{4,3},{5,4},{6,5},{7,6},{8,7},{9,8},{10,9},{11,1... | collective-permute-start | bytes 52232 | tf_op jit(solution)/shard_map/ppermute | solution.py:21
  78.4 12.2 %collective-permute-start.8 = (f32[34,1,128]{2,1,0:T(1,128)S(1)}, f32[34,1,128]{2,1,0:T(1,128)S(1)}, u32[]{:S(2)}, u32[]{:S(2)}) collective-permute-start(f32[34,1,128]{2,1,0:T(1,128)S(1)} %get-tuple-element.157), channel_id=1, source_target_pairs={{0,1},{1,2},{2,3},{3,4},{4,5},{5,6},{6,7},{7,8},{8,9},{9,10},{10,1... | collective-permute-start | bytes 52232 | tf_op jit(solution)/shard_map/ppermute | solution.py:20
  85.7 9.0 %collective-permute-start.9 = (f32[34,1,128]{2,1,0:T(1,128)S(1)}, f32[34,1,128]{2,1,0:T(1,128)S(1)}, u32[]{:S(2)}, u32[]{:S(2)}) collective-permute-start(f32[34,1,128]{2,1,0:T(1,128)S(1)} %get-tuple-element.158), channel_id=1, source_target_pairs={{1,0},{2,1},{3,2},{4,3},{5,4},{6,5},{7,6},{8,7},{9,8},{10,9},{11,1... | collective-permute-start | bytes 52232 | tf_op jit(solution)/shard_map/ppermute | solution.py:21
  87.6 26.7 %collective-permute-start.18 = (f32[1,8,64]{2,1,0:T(8,128)S(1)}, f32[1,8,64]{2,1,0:T(8,128)S(1)}, u32[]{:S(2)}, u32[]{:S(2)}) collective-permute-start(f32[1,8,64]{2,1,0:T(8,128)S(1)} %get-tuple-element.212), channel_id=1, source_target_pairs={{0,16},{16,32},{32,48},{48,64},{64,80},{80,96},{96,112},{112,128},... | collective-permute-start | bytes 6152 | tf_op jit(solution)/shard_map/ppermute | solution.py:20
  87.7 29.7 %collective-permute-start.19 = (f32[1,8,64]{2,1,0:T(8,128)S(1)}, f32[1,8,64]{2,1,0:T(8,128)S(1)}, u32[]{:S(2)}, u32[]{:S(2)}) collective-permute-start(f32[1,8,64]{2,1,0:T(8,128)S(1)} %get-tuple-element.211), channel_id=1, source_target_pairs={{16,0},{32,16},{48,32},{64,48},{80,64},{96,80},{112,96},{128,112},... | collective-permute-start | bytes 6152 | tf_op jit(solution)/shard_map/ppermute | solution.py:21
  104.3 9.0 %collective-permute-start.13 = (f32[34,1,128]{2,1,0:T(1,128)S(1)}, f32[34,1,128]{2,1,0:T(1,128)S(1)}, u32[]{:S(2)}, u32[]{:S(2)}) collective-permute-start(f32[34,1,128]{2,1,0:T(1,128)S(1)} %get-tuple-element.154), channel_id=1, source_target_pairs={{1,0},{2,1},{3,2},{4,3},{5,4},{6,5},{7,6},{8,7},{9,8},{10,9},{11,1... | collective-permute-start | bytes 52232 | tf_op jit(solution)/shard_map/ppermute | solution.py:21
  107.0 73.3 %collective-permute-start.30 = (f32[1,4,32]{2,1,0:T(4,128)S(1)}, f32[1,4,32]{2,1,0:T(4,128)S(1)}, u32[]{:S(2)}, u32[]{:S(2)}) collective-permute-start(f32[1,4,32]{2,1,0:T(4,128)S(1)} %get-tuple-element.248), channel_id=1, source_target_pairs={{0,16},{16,32},{32,48},{48,64},{64,80},{80,96},{96,112},{112,128},... | collective-permute-start | bytes 1544 | tf_op jit(solution)/shard_map/ppermute | solution.py:20
  107.1 76.2 %collective-permute-start.31 = (f32[1,4,32]{2,1,0:T(4,128)S(1)}, f32[1,4,32]{2,1,0:T(4,128)S(1)}, u32[]{:S(2)}, u32[]{:S(2)}) collective-permute-start(f32[1,4,32]{2,1,0:T(4,128)S(1)} %get-tuple-element.247), channel_id=1, source_target_pairs={{16,0},{32,16},{48,32},{64,48},{80,64},{96,80},{112,96},{128,112},... | collective-permute-start | bytes 1544 | tf_op jit(solution)/shard_map/ppermute | solution.py:21
  118.7 12.6 %collective-permute-start.16 = (f32[34,1,128]{2,1,0:T(1,128)S(1)}, f32[34,1,128]{2,1,0:T(1,128)S(1)}, u32[]{:S(2)}, u32[]{:S(2)}) collective-permute-start(f32[34,1,128]{2,1,0:T(1,128)S(1)} %get-tuple-element.151), channel_id=1, source_target_pairs={{0,1},{1,2},{2,3},{3,4},{4,5},{5,6},{6,7},{7,8},{8,9},{9,10},{10,1... | collective-permute-start | bytes 52232 | tf_op jit(solution)/shard_map/ppermute | solution.py:20
  122.0 11.3 %collective-permute-start.17 = (f32[34,1,128]{2,1,0:T(1,128)S(1)}, f32[34,1,128]{2,1,0:T(1,128)S(1)}, u32[]{:S(2)}, u32[]{:S(2)}) collective-permute-start(f32[34,1,128]{2,1,0:T(1,128)S(1)} %get-tuple-element.152), channel_id=1, source_target_pairs={{1,0},{2,1},{3,2},{4,3},{5,4},{6,5},{7,6},{8,7},{9,8},{10,9},{11,1... | collective-permute-start | bytes 52232 | tf_op jit(solution)/shard_map/ppermute | solution.py:21
  124.7 34.8 %collective-permute-start.20 = (f32[18,1,64]{2,1,0:T(1,128)S(1)}, f32[18,1,64]{2,1,0:T(1,128)S(1)}, u32[]{:S(2)}, u32[]{:S(2)}) collective-permute-start(f32[18,1,64]{2,1,0:T(1,128)S(1)} %get-tuple-element.192), channel_id=1, source_target_pairs={{0,1},{1,2},{2,3},{3,4},{4,5},{5,6},{6,7},{7,8},{8,9},{9,10},{10,1... | collective-permute-start | bytes 13832 | tf_op jit(solution)/shard_map/ppermute | solution.py:20
  131.4 28.2 %collective-permute-start.21 = (f32[18,1,64]{2,1,0:T(1,128)S(1)}, f32[18,1,64]{2,1,0:T(1,128)S(1)}, u32[]{:S(2)}, u32[]{:S(2)}) collective-permute-start(f32[18,1,64]{2,1,0:T(1,128)S(1)} %get-tuple-element.191), channel_id=1, source_target_pairs={{1,0},{2,1},{3,2},{4,3},{5,4},{6,5},{7,6},{8,7},{9,8},{10,9},{11,1... | collective-permute-start | bytes 13832 | tf_op jit(solution)/shard_map/ppermute | solution.py:21
  164.1 9.3 %collective-permute-start.24 = (f32[18,1,64]{2,1,0:T(1,128)S(1)}, f32[18,1,64]{2,1,0:T(1,128)S(1)}, u32[]{:S(2)}, u32[]{:S(2)}) collective-permute-start(f32[18,1,64]{2,1,0:T(1,128)S(1)} %get-tuple-element.189), channel_id=1, source_target_pairs={{0,1},{1,2},{2,3},{3,4},{4,5},{5,6},{6,7},{7,8},{8,9},{9,10},{10,1... | collective-permute-start | bytes 13832 | tf_op jit(solution)/shard_map/ppermute | solution.py:20
  171.3 8.9 %collective-permute-start.25 = (f32[18,1,64]{2,1,0:T(1,128)S(1)}, f32[18,1,64]{2,1,0:T(1,128)S(1)}, u32[]{:S(2)}, u32[]{:S(2)}) collective-permute-start(f32[18,1,64]{2,1,0:T(1,128)S(1)} %get-tuple-element.190), channel_id=1, source_target_pairs={{1,0},{2,1},{3,2},{4,3},{5,4},{6,5},{7,6},{8,7},{9,8},{10,9},{11,1... | collective-permute-start | bytes 13832 | tf_op jit(solution)/shard_map/ppermute | solution.py:21
  173.3 37.0 %collective-permute-start.42 = (f32[1,32,16]{1,2,0:T(8,128)}, f32[1,32,16]{1,2,0:T(8,128)}, u32[]{:S(2)}, u32[]{:S(2)}) collective-permute-start(f32[1,32,16]{1,2,0:T(8,128)} %get-tuple-element.217), channel_id=1, source_target_pairs={{0,16},{16,32},{32,48},{48,64},{64,80},{80,96},{96,112},{112,128},... | collective-permute-start | bytes 6152 | tf_op jit(solution)/shard_map/ppermute | solution.py:20
  173.3 37.0 %collective-permute-start.43 = (f32[1,32,16]{1,2,0:T(8,128)}, f32[1,32,16]{1,2,0:T(8,128)}, u32[]{:S(2)}, u32[]{:S(2)}) collective-permute-start(f32[1,32,16]{1,2,0:T(8,128)} %get-tuple-element.218), channel_id=1, source_target_pairs={{16,0},{32,16},{48,32},{64,48},{80,64},{96,80},{112,96},{128,112},... | collective-permute-start | bytes 6152 | tf_op jit(solution)/shard_map/ppermute | solution.py:21
  184.7 12.6 %collective-permute-start.28 = (f32[18,1,64]{2,1,0:T(1,128)S(1)}, f32[18,1,64]{2,1,0:T(1,128)S(1)}, u32[]{:S(2)}, u32[]{:S(2)}) collective-permute-start(f32[18,1,64]{2,1,0:T(1,128)S(1)} %get-tuple-element.187), channel_id=1, source_target_pairs={{0,1},{1,2},{2,3},{3,4},{4,5},{5,6},{6,7},{7,8},{8,9},{9,10},{10,1... | collective-permute-start | bytes 13832 | tf_op jit(solution)/shard_map/ppermute | solution.py:20
  188.0 11.4 %collective-permute-start.29 = (f32[18,1,64]{2,1,0:T(1,128)S(1)}, f32[18,1,64]{2,1,0:T(1,128)S(1)}, u32[]{:S(2)}, u32[]{:S(2)}) collective-permute-start(f32[18,1,64]{2,1,0:T(1,128)S(1)} %get-tuple-element.188), channel_id=1, source_target_pairs={{1,0},{2,1},{3,2},{4,3},{5,4},{6,5},{7,6},{8,7},{9,8},{10,9},{11,1... | collective-permute-start | bytes 13832 | tf_op jit(solution)/shard_map/ppermute | solution.py:21
  190.6 13.5 %collective-permute-start.32 = (f32[10,1,32]{2,1,0:T(1,128)}, f32[10,1,32]{2,1,0:T(1,128)}, u32[]{:S(2)}, u32[]{:S(2)}) collective-permute-start(f32[10,1,32]{2,1,0:T(1,128)} %get-tuple-element.228), channel_id=1, source_target_pairs={{0,1},{1,2},{2,3},{3,4},{4,5},{5,6},{6,7},{7,8},{8,9},{9,10},{10,1... | collective-permute-start | bytes 3848 | tf_op jit(solution)/shard_map/ppermute | solution.py:20
  197.3 9.1 %collective-permute-start.33 = (f32[10,1,32]{2,1,0:T(1,128)}, f32[10,1,32]{2,1,0:T(1,128)}, u32[]{:S(2)}, u32[]{:S(2)}) collective-permute-start(f32[10,1,32]{2,1,0:T(1,128)} %get-tuple-element.227), channel_id=1, source_target_pairs={{1,0},{2,1},{3,2},{4,3},{5,4},{6,5},{7,6},{8,7},{9,8},{10,9},{11,1... | collective-permute-start | bytes 3848 | tf_op jit(solution)/shard_map/ppermute | solution.py:21
  216.6 8.8 %collective-permute-start.37 = (f32[10,1,32]{2,1,0:T(1,128)S(1)}, f32[10,1,32]{2,1,0:T(1,128)S(1)}, u32[]{:S(2)}, u32[]{:S(2)}) collective-permute-start(f32[10,1,32]{2,1,0:T(1,128)S(1)} %get-tuple-element.226), channel_id=1, source_target_pairs={{1,0},{2,1},{3,2},{4,3},{5,4},{6,5},{7,6},{8,7},{9,8},{10,9},{11,1... | collective-permute-start | bytes 3848 | tf_op jit(solution)/shard_map/ppermute | solution.py:21
  232.5 8.8 %collective-permute-start.41 = (f32[10,1,32]{2,1,0:T(1,128)S(1)}, f32[10,1,32]{2,1,0:T(1,128)S(1)}, u32[]{:S(2)}, u32[]{:S(2)}) collective-permute-start(f32[10,1,32]{2,1,0:T(1,128)S(1)} %get-tuple-element.224), channel_id=1, source_target_pairs={{1,0},{2,1},{3,2},{4,3},{5,4},{6,5},{7,6},{8,7},{9,8},{10,9},{11,1... | collective-permute-start | bytes 3848 | tf_op jit(solution)/shard_map/ppermute | solution.py:21
  357.9 8.8 %collective-permute-start.51 = (f32[10,1,32]{2,1,0:T(1,128)S(1)}, f32[10,1,32]{2,1,0:T(1,128)S(1)}, u32[]{:S(2)}, u32[]{:S(2)}) collective-permute-start(f32[10,1,32]{2,1,0:T(1,128)S(1)} %get-tuple-element.220), channel_id=1, source_target_pairs={{1,0},{2,1},{3,2},{4,3},{5,4},{6,5},{7,6},{8,7},{9,8},{10,9},{11,1... | collective-permute-start | bytes 3848 | tf_op jit(solution)/shard_map/ppermute | solution.py:21
  374.2 8.9 %collective-permute-start.55 = (f32[18,1,64]{2,1,0:T(1,128)S(1)}, f32[18,1,64]{2,1,0:T(1,128)S(1)}, u32[]{:S(2)}, u32[]{:S(2)}) collective-permute-start(f32[18,1,64]{2,1,0:T(1,128)S(1)} %get-tuple-element.186), channel_id=1, source_target_pairs={{1,0},{2,1},{3,2},{4,3},{5,4},{6,5},{7,6},{8,7},{9,8},{10,9},{11,1... | collective-permute-start | bytes 13832 | tf_op jit(solution)/shard_map/ppermute | solution.py:21
  390.5 8.9 %collective-permute-start.59 = (f32[18,1,64]{2,1,0:T(1,128)S(1)}, f32[18,1,64]{2,1,0:T(1,128)S(1)}, u32[]{:S(2)}, u32[]{:S(2)}) collective-permute-start(f32[18,1,64]{2,1,0:T(1,128)S(1)} %get-tuple-element.184), channel_id=1, source_target_pairs={{1,0},{2,1},{3,2},{4,3},{5,4},{6,5},{7,6},{8,7},{9,8},{10,9},{11,1... | collective-permute-start | bytes 13832 | tf_op jit(solution)/shard_map/ppermute | solution.py:21
  407.7 9.0 %collective-permute-start.63 = (f32[34,1,128]{2,1,0:T(1,128)S(1)}, f32[34,1,128]{2,1,0:T(1,128)S(1)}, u32[]{:S(2)}, u32[]{:S(2)}) collective-permute-start(f32[34,1,128]{2,1,0:T(1,128)S(1)} %get-tuple-element.150), channel_id=1, source_target_pairs={{1,0},{2,1},{3,2},{4,3},{5,4},{6,5},{7,6},{8,7},{9,8},{10,9},{11,1... | collective-permute-start | bytes 52232 | tf_op jit(solution)/shard_map/ppermute | solution.py:21
  423.4 9.0 %collective-permute-start.67 = (f32[34,1,128]{2,1,0:T(1,128)S(1)}, f32[34,1,128]{2,1,0:T(1,128)S(1)}, u32[]{:S(2)}, u32[]{:S(2)}) collective-permute-start(f32[34,1,128]{2,1,0:T(1,128)S(1)} %get-tuple-element.148), channel_id=1, source_target_pairs={{1,0},{2,1},{3,2},{4,3},{5,4},{6,5},{7,6},{8,7},{9,8},{10,9},{11,1... | collective-permute-start | bytes 52232 | tf_op jit(solution)/shard_map/ppermute | solution.py:21
  (92 other events, 2154.1 us)
where the time goes:
time: 436 us; the launch traced here: 433 us
  starting transfers between devices  209 us (48%)
  waiting for transfers between devices  90.6 us (21%)
  local copies, waits for them, and re-layouts  49.2 us (11%)
  blocking collectives  41.7 us (10%)
  other arithmetic  40.7 us (9%)
    ppermute x48, starting transfers between devices, padded_2(): after = lax.ppermute(first, axis, down)  145 us
    ppermute x48, starting transfers between devices, padded_2(): before = lax.ppermute(last, axis, up)  64.2 us
    ppermute x48, waiting for transfers between devices, padded_2(): after = lax.ppermute(first, axis, down)  57.3 us
    reshape x4, local copies, waits for them, and re-layouts, coarsen(): field.reshape(size_x // 2, 2, size_y // 2, 2, size_z // 2, 2)  40.2 us
    ppermute x48, waiting for transfers between devices, padded_2(): before = lax.ppermute(last, axis, up)  33.3 us
    all_gather x1, blocking collectives, on_device(): lax.all_gather(coarse_perm, 'col', axis=1, tiled=True)  21.4 us
    all_gather x1, blocking collectives, on_device(): lax.all_gather(right_side, 'col', axis=1, tiled=True)  20.3 us
    reduce_sum x6, other arithmetic, coarsen(): field.reshape(size_x // 2, 2, size_y // 2, 2, size_z // 2, 2)  15.3 us
  transfers between devices with their start and end apart: 96, of which 39 were waited for; matrix products, arithmetic and copies ran while one was open for 18% of the time, Pallas kernels for 0%

commit v1 on v0

--- a/solution.py
+++ b/solution.py
@@ -8,6 +8,22 @@
 NU2 = 2
 CSWEEPS = 16
 OMEGA = 0.8
+
+
+def gather_around(x, axis, dim):
+    ways, here, step = (lax.axis_size(axis), lax.axis_index(axis), x.shape[dim])
+    shape = [n * ways if d == dim else n for d, n in enumerate(x.shape)]
+    full = lax.dynamic_update_slice_in_dim(jnp.zeros(shape, x.dtype), x, here * step, axis=dim)
+    going_up = going_down = x
+    for far in range(1, ways // 2 + 1):
+        going_up = lax.ppermute(going_up, axis, [(d, (d + 1) % ways) for d in range(ways)])
+        full = lax.dynamic_update_slice_in_dim(full, going_up, (here - far) % ways * step, axis=dim)
+        if 2 * far < ways:
+            going_down = lax.ppermute(going_down, axis, [(d, (d - 1) % ways) for d in range(ways)])
+            full = lax.dynamic_update_slice_in_dim(
+                full, going_down, (here + far) % ways * step, axis=dim
+            )
+    return full
 
 
 def padded_2(array, sides, width):
@@ -123,7 +139,7 @@
     size_x, size_y, size_z = right_side.shape
     coarse_scale = 0.25**LEVELS
     band_rhs, band_perm = (
-        lax.all_gather(right_side, "col", axis=1, tiled=True),
+        gather_around(right_side, "col", 1),
         lax.all_gather(coarse_perm, "col", axis=1, tiled=True),
     )
     band_faces = coefficients(band_perm_pad(band_perm), band_perm, coarse_scale)

time: 436 us -> 492 us (1.13)
  starting transfers between devices: 209 us -> 274 us
  blocking collectives: 41.7 us -> 21.4 us
  local copies, waits for them, and re-layouts: 49.2 us -> 60.5 us
    ppermute x0 -> x15, starting transfers between devices: none -> 66.1 us  [the longest x8 50.6 us: gather_around(): lax.ppermute(going_up, axis, [(d, (d + 1) % ways) for d in range(ways)])]
    all_gather x1 -> x0, blocking collectives: 20.3 us -> none  [on_device(): lax.all_gather(right_side, 'col', axis=1, tiled=True)]
    dynamic_update_slice x0 -> x16, local copies, waits for them, and re-layouts: none -> 11 us  [the longest x8 5.72 us: gather_around(): lax.dynamic_update_slice_in_dim(full, going_up, (here - far) % ways * ste...]
  transfers between devices with their start and end apart: 96 -> 111, of which waited for: 39 -> 39; matrix products, arithmetic and copies ran while one was open for 18% -> 18% of each run, Pallas kernels for 0% -> 0%
where the time goes in v1:
time: 492 us; the launch traced here: 490 us
  starting transfers between devices  274 us (56%)
  waiting for transfers between devices  90.7 us (18%)
  local copies, waits for them, and re-layouts  60.5 us (12%)
  other arithmetic  40.8 us (8%)
  blocking collectives  21.4 us (4%)
    ppermute x48, starting transfers between devices, padded_2(): after = lax.ppermute(first, axis, down)  146 us
    ppermute x48, starting transfers between devices, padded_2(): before = lax.ppermute(last, axis, up)  61.8 us
    ppermute x48, waiting for transfers between devices, padded_2(): after = lax.ppermute(first, axis, down)  55.9 us
    ppermute x8, starting transfers between devices, gather_around(): lax.ppermute(going_up, axis, [(d, (d + 1) % ways) for d in range(ways)])  50.6 us
    reshape x4, local copies, waits for them, and re-layouts, coarsen(): field.reshape(size_x // 2, 2, size_y // 2, 2, size_z // 2, 2)  40.2 us
    ppermute x48, waiting for transfers between devices, padded_2(): before = lax.ppermute(last, axis, up)  34.8 us
    all_gather x1, blocking collectives, on_device(): lax.all_gather(coarse_perm, 'col', axis=1, tiled=True)  21.4 us
    ppermute x7, starting transfers between devices, gather_around(): lax.ppermute(going_down, axis, [(d, (d - 1) % ways) for d in range(ways)])  15.4 us
  transfers between devices with their start and end apart: 111, of which 39 were waited for; matrix products, arithmetic and copies ran while one was open for 18% of the time, Pallas kernels for 0%

profile of v1, /device:TPU:30, one launch (start us, length us, event | category | flops | bytes accessed | tf_op | source)
XLA Modules:
  0.0 490.0 jit_solution(17432380541616120774)
XLA Ops:
  0.7 8.9 %collective-permute-start.3 = (f32[1,16,128]{2,1,0:T(8,128)S(1)}, f32[1,16,128]{2,1,0:T(8,128)S(1)}, u32[]{:S(2)}, u32[]{:S(2)}) collective-permute-start(f32[1,16,128]{2,1,0:T(8,128)S(1)} %get-tuple-element.167), channel_id=1, source_target_pairs={{16,0},{32,16},{48,32},{64,48},{80,64},{96,80},{112,96},{128,112},... | collective-permute-start | bytes 24584 | tf_op jit(solution)/shard_map/ppermute | solution.py:37
  17.5 18.9 %reshape.48 = f32[16,2,8,2,64,2]{5,4,3,2,1,0:T(8,128)} reshape(f32[32,16,128]{2,1,0:T(8,128)} %param.7) | data formatting | bytes 524288 | tf_op jit(solution)/shard_map/reshape | solution.py:82
  36.4 7.0 %reduce_sum.55 = f32[16,8,64]{2,1,0:T(8,128)S(1)} reduce(f32[16,2,8,2,64,2]{5,4,3,2,1,0:T(8,128)} %reshape.48, f32[]{:T(128)} %constant.145.clone.1), dimensions={1,3,5}, to_apply=%region_1.0 | reduce | flops 57344 | bytes 294916 | tf_op jit(solution)/shard_map/reduce_sum | solution.py:82
  49.1 21.4 %all_gather.3 = f32[4,32,16]{2,0,1:T(4,128)S(1)} all-gather(f32[4,2,16]{2,0,1:T(4,128)S(1)} %copy.509), channel_id=1, replica_groups=mesh['row'=32,'col'=16] {'col'}, dimensions={1}, use_global_device_ids=true | all-gather | bytes 8704 | tf_op jit(solution)/shard_map/all_gather | solution.py:143
  72.6 4.6 collective-permute-start.4
  79.2 7.2 %collective-permute-start.8 = (f32[34,1,128]{2,1,0:T(1,128)S(1)}, f32[34,1,128]{2,1,0:T(1,128)S(1)}, u32[]{:S(2)}, u32[]{:S(2)}) collective-permute-start(f32[34,1,128]{2,1,0:T(1,128)S(1)} %get-tuple-element.147), channel_id=1, source_target_pairs={{0,1},{1,2},{2,3},{3,4},{4,5},{5,6},{6,7},{7,8},{8,9},{9,10},{10,1... | collective-permute-start | bytes 52232 | tf_op jit(solution)/shard_map/ppermute | solution.py:36
  91.4 4.0 collective-permute-done.9
  125.5 6.6 %collective-permute-start.20 = (f32[18,1,64]{2,1,0:T(1,128)S(1)}, f32[18,1,64]{2,1,0:T(1,128)S(1)}, u32[]{:S(2)}, u32[]{:S(2)}) collective-permute-start(f32[18,1,64]{2,1,0:T(1,128)S(1)} %get-tuple-element.182), channel_id=1, source_target_pairs={{0,1},{1,2},{2,3},{3,4},{4,5},{5,6},{6,7},{7,8},{8,9},{9,10},{10,1... | collective-permute-start | bytes 13832 | tf_op jit(solution)/shard_map/ppermute | solution.py:36
  135.2 18.1 %reshape.47 = f32[16,2,8,2,64,2]{5,4,3,2,1,0:T(8,128)} reshape(f32[32,16,128]{2,1,0:T(8,128)S(1)} %fusion.47) | data formatting | bytes 524288 | tf_op jit(solution)/shard_map/reshape | solution.py:82
  153.3 7.0 %reduce_sum.54 = f32[16,8,64]{2,1,0:T(8,128)S(1)} reduce(f32[16,2,8,2,64,2]{5,4,3,2,1,0:T(8,128)} %reshape.47, f32[]{:T(128)} %constant.145.clone.1), dimensions={1,3,5}, to_apply=%region_0.0 | reduce | flops 57344 | bytes 294916 | tf_op jit(solution)/shard_map/reduce_sum | solution.py:82
  164.9 7.2 %collective-permute-start.24 = (f32[18,1,64]{2,1,0:T(1,128)S(1)}, f32[18,1,64]{2,1,0:T(1,128)S(1)}, u32[]{:S(2)}, u32[]{:S(2)}) collective-permute-start(f32[18,1,64]{2,1,0:T(1,128)S(1)} %get-tuple-element.179), channel_id=1, source_target_pairs={{0,1},{1,2},{2,3},{3,4},{4,5},{5,6},{6,7},{7,8},{8,9},{9,10},{10,1... | collective-permute-start | bytes 13832 | tf_op jit(solution)/shard_map/ppermute | solution.py:36
  191.4 6.7 %collective-permute-start.32 = (f32[10,1,32]{2,1,0:T(1,128)}, f32[10,1,32]{2,1,0:T(1,128)}, u32[]{:S(2)}, u32[]{:S(2)}) collective-permute-start(f32[10,1,32]{2,1,0:T(1,128)} %get-tuple-element.218), channel_id=1, source_target_pairs={{0,1},{1,2},{2,3},{3,4},{4,5},{5,6},{6,7},{7,8},{8,9},{9,10},{10,1... | collective-permute-start | bytes 3848 | tf_op jit(solution)/shard_map/ppermute | solution.py:36
  212.5 4.9 %collective-permute-start.36 = (f32[10,1,32]{2,1,0:T(1,128)S(1)}, f32[10,1,32]{2,1,0:T(1,128)S(1)}, u32[]{:S(2)}, u32[]{:S(2)}) collective-permute-start(f32[10,1,32]{2,1,0:T(1,128)S(1)} %get-tuple-element.215), channel_id=1, source_target_pairs={{0,1},{1,2},{2,3},{3,4},{4,5},{5,6},{6,7},{7,8},{8,9},{9,10},{10,1... | collective-permute-start | bytes 3848 | tf_op jit(solution)/shard_map/ppermute | solution.py:36
  219.4 6.8 %collective-permute-done.37 = f32[10,1,32]{2,1,0:T(1,128)S(1)} collective-permute-done((f32[10,1,32]{2,1,0:T(1,128)S(1)}, f32[10,1,32]{2,1,0:T(1,128)S(1)}, u32[]{:S(2)}, u32[]{:S(2)}) %collective-permute-start.37) | collective-permute-done | bytes 1312 | tf_op jit(solution)/shard_map/ppermute | solution.py:37
  233.3 3.9 collective-permute-start.41
  237.3 4.8 collective-permute-done.41
  245.3 3.9 collective-permute-start.43
  249.2 5.2 %collective-permute-start.44 = (f32[4,2,16]{1,2,0:T(8,128)S(1)}, f32[4,2,16]{1,2,0:T(8,128)S(1)}, u32[]{:S(2)}, u32[]{:S(2)}) collective-permute-start(f32[4,2,16]{1,2,0:T(8,128)S(1)} %collective-permute-done.42), channel_id=1, source_target_pairs={{0,1},{1,2},{2,3},{3,4},{4,5},{5,6},{6,7},{7,8},{8,9},{9,10},{10,1... | collective-permute-start | bytes 1544 | tf_op jit(solution)/shard_map/ppermute | solution.py:19
  256.4 7.2 %collective-permute-start.46 = (f32[4,2,16]{1,2,0:T(8,128)S(1)}, f32[4,2,16]{1,2,0:T(8,128)S(1)}, u32[]{:S(2)}, u32[]{:S(2)}) collective-permute-start(f32[4,2,16]{1,2,0:T(8,128)S(1)} %collective-permute-done.44), channel_id=1, source_target_pairs={{0,1},{1,2},{2,3},{3,4},{4,5},{5,6},{6,7},{7,8},{8,9},{9,10},{10,1... | collective-permute-start | bytes 1544 | tf_op jit(solution)/shard_map/ppermute | solution.py:19
  265.6 7.2 %collective-permute-start.48 = (f32[4,2,16]{1,2,0:T(8,128)S(1)}, f32[4,2,16]{1,2,0:T(8,128)S(1)}, u32[]{:S(2)}, u32[]{:S(2)}) collective-permute-start(f32[4,2,16]{1,2,0:T(8,128)S(1)} %collective-permute-done.46), channel_id=1, source_target_pairs={{0,1},{1,2},{2,3},{3,4},{4,5},{5,6},{6,7},{7,8},{8,9},{9,10},{10,1... | collective-permute-start | bytes 1544 | tf_op jit(solution)/shard_map/ppermute | solution.py:19
  274.9 7.2 %collective-permute-start.50 = (f32[4,2,16]{1,2,0:T(8,128)S(1)}, f32[4,2,16]{1,2,0:T(8,128)S(1)}, u32[]{:S(2)}, u32[]{:S(2)}) collective-permute-start(f32[4,2,16]{1,2,0:T(8,128)S(1)} %collective-permute-done.48), channel_id=1, source_target_pairs={{0,1},{1,2},{2,3},{3,4},{4,5},{5,6},{6,7},{7,8},{8,9},{9,10},{10,1... | collective-permute-start | bytes 1544 | tf_op jit(solution)/shard_map/ppermute | solution.py:19
  284.1 7.2 %collective-permute-start.52 = (f32[4,2,16]{1,2,0:T(8,128)S(1)}, f32[4,2,16]{1,2,0:T(8,128)S(1)}, u32[]{:S(2)}, u32[]{:S(2)}) collective-permute-start(f32[4,2,16]{1,2,0:T(8,128)S(1)} %collective-permute-done.50), channel_id=1, source_target_pairs={{0,1},{1,2},{2,3},{3,4},{4,5},{5,6},{6,7},{7,8},{8,9},{9,10},{10,1... | collective-permute-start | bytes 1544 | tf_op jit(solution)/shard_map/ppermute | solution.py:19
  294.1 7.2 %collective-permute-start.54 = (f32[4,2,16]{1,2,0:T(8,128)S(1)}, f32[4,2,16]{1,2,0:T(8,128)S(1)}, u32[]{:S(2)}, u32[]{:S(2)}) collective-permute-start(f32[4,2,16]{1,2,0:T(8,128)S(1)} %collective-permute-done.52), channel_id=1, source_target_pairs={{0,1},{1,2},{2,3},{3,4},{4,5},{5,6},{6,7},{7,8},{8,9},{9,10},{10,1... | collective-permute-start | bytes 1544 | tf_op jit(solution)/shard_map/ppermute | solution.py:19
  307.2 7.2 %collective-permute-start.56 = (f32[4,2,16]{1,2,0:T(8,128)S(1)}, f32[4,2,16]{1,2,0:T(8,128)S(1)}, u32[]{:S(2)}, u32[]{:S(2)}) collective-permute-start(f32[4,2,16]{1,2,0:T(8,128)S(1)} %collective-permute-done.54), channel_id=1, source_target_pairs={{0,1},{1,2},{2,3},{3,4},{4,5},{5,6},{6,7},{7,8},{8,9},{9,10},{10,1... | collective-permute-start | bytes 1544 | tf_op jit(solution)/shard_map/ppermute | solution.py:19
  322.8 68.6 %while.10 = (s32[]{:T(128)}, f32[4,32,16]{1,2,0:T(8,128)S(1)}, f32[4,32,16]{1,2,0:T(8,128)S(1)}, f32[4,32,16]{1,2,0:T(8,128)S(1)}, f32[4,32,16]{1,2,0:T(8,128)S(...) while((s32[]{:T(128)}, f32[4,32,16]{1,2,0:T(8,128)S(1)}, ...), condition=%wide.region_7.8_spmd, body=%wide.region_6.7_spmd.sunk | while | flops 43010 | bytes 279997 | solution.py:113
  402.0 5.5 %collective-permute-done.62 = f32[10,1,32]{2,1,0:T(1,128)S(1)} collective-permute-done((f32[10,1,32]{2,1,0:T(1,128)S(1)}, f32[10,1,32]{2,1,0:T(1,128)S(1)}, u32[]{:S(2)}, u32[]{:S(2)}) %collective-permute-start.62) | collective-permute-done | bytes 1312 | tf_op jit(solution)/shard_map/ppermute | solution.py:37
  414.5 3.9 collective-permute-start.66
  418.5 4.8 collective-permute-done.66
  434.8 4.9 collective-permute-done.70
  451.0 4.9 collective-permute-done.74
  468.4 4.9 collective-permute-done.78
  484.1 4.9 collective-permute-done.82
  (505 shorter events, 263.0 us)
Async XLA Ops:
  0.7 71.7 %collective-permute-start.2 = (f32[1,16,128]{2,1,0:T(8,128)S(1)}, f32[1,16,128]{2,1,0:T(8,128)S(1)}, u32[]{:S(2)}, u32[]{:S(2)}) collective-permute-start(f32[1,16,128]{2,1,0:T(8,128)S(1)} %get-tuple-element.168), channel_id=1, source_target_pairs={{0,16},{16,32},{32,48},{48,64},{64,80},{80,96},{96,112},{112,128},... | collective-permute-start | bytes 24584 | tf_op jit(solution)/shard_map/ppermute | solution.py:36
  0.7 71.8 %collective-permute-start.3 = (f32[1,16,128]{2,1,0:T(8,128)S(1)}, f32[1,16,128]{2,1,0:T(8,128)S(1)}, u32[]{:S(2)}, u32[]{:S(2)}) collective-permute-start(f32[1,16,128]{2,1,0:T(8,128)S(1)} %get-tuple-element.167), channel_id=1, source_target_pairs={{16,0},{32,16},{48,32},{64,48},{80,64},{96,80},{112,96},{128,112},... | collective-permute-start | bytes 24584 | tf_op jit(solution)/shard_map/ppermute | solution.py:37
  10.4 68.7 %collective-permute-start.6 = (f32[1,16,128]{2,1,0:T(8,128)S(1)}, f32[1,16,128]{2,1,0:T(8,128)S(1)}, u32[]{:S(2)}, u32[]{:S(2)}) collective-permute-start(f32[1,16,128]{2,1,0:T(8,128)S(1)} %get-tuple-element.172), channel_id=1, source_target_pairs={{0,16},{16,32},{32,48},{48,64},{64,80},{80,96},{96,112},{112,128},... | collective-permute-start | bytes 24584 | tf_op jit(solution)/shard_map/ppermute | solution.py:36
  10.4 68.8 %collective-permute-start.7 = (f32[1,16,128]{2,1,0:T(8,128)S(1)}, f32[1,16,128]{2,1,0:T(8,128)S(1)}, u32[]{:S(2)}, u32[]{:S(2)}) collective-permute-start(f32[1,16,128]{2,1,0:T(8,128)S(1)} %get-tuple-element.171), channel_id=1, source_target_pairs={{16,0},{32,16},{48,32},{64,48},{80,64},{96,80},{112,96},{128,112},... | collective-permute-start | bytes 24584 | tf_op jit(solution)/shard_map/ppermute | solution.py:37
  72.6 15.9 %collective-permute-start.4 = (f32[34,1,128]{2,1,0:T(1,128)S(1)}, f32[34,1,128]{2,1,0:T(1,128)S(1)}, u32[]{:S(2)}, u32[]{:S(2)}) collective-permute-start(f32[34,1,128]{2,1,0:T(1,128)S(1)} %get-tuple-element.146), channel_id=1, source_target_pairs={{0,1},{1,2},{2,3},{3,4},{4,5},{5,6},{6,7},{7,8},{8,9},{9,10},{10,1... | collective-permute-start | bytes 52232 | tf_op jit(solution)/shard_map/ppermute | solution.py:36
  77.2 14.2 %collective-permute-start.5 = (f32[34,1,128]{2,1,0:T(1,128)S(1)}, f32[34,1,128]{2,1,0:T(1,128)S(1)}, u32[]{:S(2)}, u32[]{:S(2)}) collective-permute-start(f32[34,1,128]{2,1,0:T(1,128)S(1)} %get-tuple-element.145), channel_id=1, source_target_pairs={{1,0},{2,1},{3,2},{4,3},{5,4},{6,5},{7,6},{8,7},{9,8},{10,9},{11,1... | collective-permute-start | bytes 52232 | tf_op jit(solution)/shard_map/ppermute | solution.py:37
  79.2 12.2 %collective-permute-start.8 = (f32[34,1,128]{2,1,0:T(1,128)S(1)}, f32[34,1,128]{2,1,0:T(1,128)S(1)}, u32[]{:S(2)}, u32[]{:S(2)}) collective-permute-start(f32[34,1,128]{2,1,0:T(1,128)S(1)} %get-tuple-element.147), channel_id=1, source_target_pairs={{0,1},{1,2},{2,3},{3,4},{4,5},{5,6},{6,7},{7,8},{8,9},{9,10},{10,1... | collective-permute-start | bytes 52232 | tf_op jit(solution)/shard_map/ppermute | solution.py:36
  88.4 26.7 %collective-permute-start.18 = (f32[1,8,64]{2,1,0:T(8,128)S(1)}, f32[1,8,64]{2,1,0:T(8,128)S(1)}, u32[]{:S(2)}, u32[]{:S(2)}) collective-permute-start(f32[1,8,64]{2,1,0:T(8,128)S(1)} %get-tuple-element.202), channel_id=1, source_target_pairs={{0,16},{16,32},{32,48},{48,64},{64,80},{80,96},{96,112},{112,128},... | collective-permute-start | bytes 6152 | tf_op jit(solution)/shard_map/ppermute | solution.py:36
  88.5 29.7 %collective-permute-start.19 = (f32[1,8,64]{2,1,0:T(8,128)S(1)}, f32[1,8,64]{2,1,0:T(8,128)S(1)}, u32[]{:S(2)}, u32[]{:S(2)}) collective-permute-start(f32[1,8,64]{2,1,0:T(8,128)S(1)} %get-tuple-element.201), channel_id=1, source_target_pairs={{16,0},{32,16},{48,32},{64,48},{80,64},{96,80},{112,96},{128,112},... | collective-permute-start | bytes 6152 | tf_op jit(solution)/shard_map/ppermute | solution.py:37
  107.9 73.3 %collective-permute-start.30 = (f32[1,4,32]{2,1,0:T(4,128)S(1)}, f32[1,4,32]{2,1,0:T(4,128)S(1)}, u32[]{:S(2)}, u32[]{:S(2)}) collective-permute-start(f32[1,4,32]{2,1,0:T(4,128)S(1)} %get-tuple-element.238), channel_id=1, source_target_pairs={{0,16},{16,32},{32,48},{48,64},{64,80},{80,96},{96,112},{112,128},... | collective-permute-start | bytes 1544 | tf_op jit(solution)/shard_map/ppermute | solution.py:36
  107.9 76.2 %collective-permute-start.31 = (f32[1,4,32]{2,1,0:T(4,128)S(1)}, f32[1,4,32]{2,1,0:T(4,128)S(1)}, u32[]{:S(2)}, u32[]{:S(2)}) collective-permute-start(f32[1,4,32]{2,1,0:T(4,128)S(1)} %get-tuple-element.237), channel_id=1, source_target_pairs={{16,0},{32,16},{48,32},{64,48},{80,64},{96,80},{112,96},{128,112},... | collective-permute-start | bytes 1544 | tf_op jit(solution)/shard_map/ppermute | solution.py:37
  119.5 12.6 %collective-permute-start.16 = (f32[34,1,128]{2,1,0:T(1,128)S(1)}, f32[34,1,128]{2,1,0:T(1,128)S(1)}, u32[]{:S(2)}, u32[]{:S(2)}) collective-permute-start(f32[34,1,128]{2,1,0:T(1,128)S(1)} %get-tuple-element.141), channel_id=1, source_target_pairs={{0,1},{1,2},{2,3},{3,4},{4,5},{5,6},{6,7},{7,8},{8,9},{9,10},{10,1... | collective-permute-start | bytes 52232 | tf_op jit(solution)/shard_map/ppermute | solution.py:36
  122.8 11.3 %collective-permute-start.17 = (f32[34,1,128]{2,1,0:T(1,128)S(1)}, f32[34,1,128]{2,1,0:T(1,128)S(1)}, u32[]{:S(2)}, u32[]{:S(2)}) collective-permute-start(f32[34,1,128]{2,1,0:T(1,128)S(1)} %get-tuple-element.142), channel_id=1, source_target_pairs={{1,0},{2,1},{3,2},{4,3},{5,4},{6,5},{7,6},{8,7},{9,8},{10,9},{11,1... | collective-permute-start | bytes 52232 | tf_op jit(solution)/shard_map/ppermute | solution.py:37
  125.5 34.8 %collective-permute-start.20 = (f32[18,1,64]{2,1,0:T(1,128)S(1)}, f32[18,1,64]{2,1,0:T(1,128)S(1)}, u32[]{:S(2)}, u32[]{:S(2)}) collective-permute-start(f32[18,1,64]{2,1,0:T(1,128)S(1)} %get-tuple-element.182), channel_id=1, source_target_pairs={{0,1},{1,2},{2,3},{3,4},{4,5},{5,6},{6,7},{7,8},{8,9},{9,10},{10,1... | collective-permute-start | bytes 13832 | tf_op jit(solution)/shard_map/ppermute | solution.py:36
  132.2 28.2 %collective-permute-start.21 = (f32[18,1,64]{2,1,0:T(1,128)S(1)}, f32[18,1,64]{2,1,0:T(1,128)S(1)}, u32[]{:S(2)}, u32[]{:S(2)}) collective-permute-start(f32[18,1,64]{2,1,0:T(1,128)S(1)} %get-tuple-element.181), channel_id=1, source_target_pairs={{1,0},{2,1},{3,2},{4,3},{5,4},{6,5},{7,6},{8,7},{9,8},{10,9},{11,1... | collective-permute-start | bytes 13832 | tf_op jit(solution)/shard_map/ppermute | solution.py:37
  164.9 9.3 %collective-permute-start.24 = (f32[18,1,64]{2,1,0:T(1,128)S(1)}, f32[18,1,64]{2,1,0:T(1,128)S(1)}, u32[]{:S(2)}, u32[]{:S(2)}) collective-permute-start(f32[18,1,64]{2,1,0:T(1,128)S(1)} %get-tuple-element.179), channel_id=1, source_target_pairs={{0,1},{1,2},{2,3},{3,4},{4,5},{5,6},{6,7},{7,8},{8,9},{9,10},{10,1... | collective-permute-start | bytes 13832 | tf_op jit(solution)/shard_map/ppermute | solution.py:36
  174.1 117.2 %collective-permute-start.57 = (f32[1,32,16]{1,2,0:T(8,128)}, f32[1,32,16]{1,2,0:T(8,128)}, u32[]{:S(2)}, u32[]{:S(2)}) collective-permute-start(f32[1,32,16]{1,2,0:T(8,128)} %get-tuple-element.207), channel_id=1, source_target_pairs={{0,16},{16,32},{32,48},{48,64},{64,80},{80,96},{96,112},{112,128},... | collective-permute-start | bytes 6152 | tf_op jit(solution)/shard_map/ppermute | solution.py:36
  174.2 117.2 %collective-permute-start.58 = (f32[1,32,16]{1,2,0:T(8,128)}, f32[1,32,16]{1,2,0:T(8,128)}, u32[]{:S(2)}, u32[]{:S(2)}) collective-permute-start(f32[1,32,16]{1,2,0:T(8,128)} %get-tuple-element.208), channel_id=1, source_target_pairs={{16,0},{32,16},{48,32},{64,48},{80,64},{96,80},{112,96},{128,112},... | collective-permute-start | bytes 6152 | tf_op jit(solution)/shard_map/ppermute | solution.py:37
  185.5 12.6 %collective-permute-start.28 = (f32[18,1,64]{2,1,0:T(1,128)S(1)}, f32[18,1,64]{2,1,0:T(1,128)S(1)}, u32[]{:S(2)}, u32[]{:S(2)}) collective-permute-start(f32[18,1,64]{2,1,0:T(1,128)S(1)} %get-tuple-element.177), channel_id=1, source_target_pairs={{0,1},{1,2},{2,3},{3,4},{4,5},{5,6},{6,7},{7,8},{8,9},{9,10},{10,1... | collective-permute-start | bytes 13832 | tf_op jit(solution)/shard_map/ppermute | solution.py:36
  188.8 11.4 %collective-permute-start.29 = (f32[18,1,64]{2,1,0:T(1,128)S(1)}, f32[18,1,64]{2,1,0:T(1,128)S(1)}, u32[]{:S(2)}, u32[]{:S(2)}) collective-permute-start(f32[18,1,64]{2,1,0:T(1,128)S(1)} %get-tuple-element.178), channel_id=1, source_target_pairs={{1,0},{2,1},{3,2},{4,3},{5,4},{6,5},{7,6},{8,7},{9,8},{10,9},{11,1... | collective-permute-start | bytes 13832 | tf_op jit(solution)/shard_map/ppermute | solution.py:37
  191.4 13.5 %collective-permute-start.32 = (f32[10,1,32]{2,1,0:T(1,128)}, f32[10,1,32]{2,1,0:T(1,128)}, u32[]{:S(2)}, u32[]{:S(2)}) collective-permute-start(f32[10,1,32]{2,1,0:T(1,128)} %get-tuple-element.218), channel_id=1, source_target_pairs={{0,1},{1,2},{2,3},{3,4},{4,5},{5,6},{6,7},{7,8},{8,9},{9,10},{10,1... | collective-permute-start | bytes 3848 | tf_op jit(solution)/shard_map/ppermute | solution.py:36
  245.3 9.2 %collective-permute-start.43 = (f32[4,2,16]{1,2,0:T(8,128)S(1)}, f32[4,2,16]{1,2,0:T(8,128)S(1)}, u32[]{:S(2)}, u32[]{:S(2)}) collective-permute-start(f32[4,2,16]{1,2,0:T(8,128)S(1)} %broadcast_multiply_fusion.2), channel_id=1, source_target_pairs={{0,15},{1,0},{2,1},{3,2},{4,3},{5,4},{6,5},{7,6},{8,7},{9,8},{10,9... | collective-permute-start | bytes 1544 | tf_op jit(solution)/shard_map/ppermute | solution.py:22
  263.7 9.2 %collective-permute-start.47 = (f32[4,2,16]{1,2,0:T(8,128)S(1)}, f32[4,2,16]{1,2,0:T(8,128)S(1)}, u32[]{:S(2)}, u32[]{:S(2)}) collective-permute-start(f32[4,2,16]{1,2,0:T(8,128)S(1)} %collective-permute-done.45), channel_id=1, source_target_pairs={{0,15},{1,0},{2,1},{3,2},{4,3},{5,4},{6,5},{7,6},{8,7},{9,8},{10,9... | collective-permute-start | bytes 1544 | tf_op jit(solution)/shard_map/ppermute | solution.py:22
  265.6 9.2 %collective-permute-start.48 = (f32[4,2,16]{1,2,0:T(8,128)S(1)}, f32[4,2,16]{1,2,0:T(8,128)S(1)}, u32[]{:S(2)}, u32[]{:S(2)}) collective-permute-start(f32[4,2,16]{1,2,0:T(8,128)S(1)} %collective-permute-done.46), channel_id=1, source_target_pairs={{0,1},{1,2},{2,3},{3,4},{4,5},{5,6},{6,7},{7,8},{8,9},{9,10},{10,1... | collective-permute-start | bytes 1544 | tf_op jit(solution)/shard_map/ppermute | solution.py:19
  272.9 9.2 %collective-permute-start.49 = (f32[4,2,16]{1,2,0:T(8,128)S(1)}, f32[4,2,16]{1,2,0:T(8,128)S(1)}, u32[]{:S(2)}, u32[]{:S(2)}) collective-permute-start(f32[4,2,16]{1,2,0:T(8,128)S(1)} %collective-permute-done.47), channel_id=1, source_target_pairs={{0,15},{1,0},{2,1},{3,2},{4,3},{5,4},{6,5},{7,6},{8,7},{9,8},{10,9... | collective-permute-start | bytes 1544 | tf_op jit(solution)/shard_map/ppermute | solution.py:22
  274.9 9.2 %collective-permute-start.50 = (f32[4,2,16]{1,2,0:T(8,128)S(1)}, f32[4,2,16]{1,2,0:T(8,128)S(1)}, u32[]{:S(2)}, u32[]{:S(2)}) collective-permute-start(f32[4,2,16]{1,2,0:T(8,128)S(1)} %collective-permute-done.48), channel_id=1, source_target_pairs={{0,1},{1,2},{2,3},{3,4},{4,5},{5,6},{6,7},{7,8},{8,9},{9,10},{10,1... | collective-permute-start | bytes 1544 | tf_op jit(solution)/shard_map/ppermute | solution.py:19
  282.2 10.0 %collective-permute-start.51 = (f32[4,2,16]{1,2,0:T(8,128)S(1)}, f32[4,2,16]{1,2,0:T(8,128)S(1)}, u32[]{:S(2)}, u32[]{:S(2)}) collective-permute-start(f32[4,2,16]{1,2,0:T(8,128)S(1)} %collective-permute-done.49), channel_id=1, source_target_pairs={{0,15},{1,0},{2,1},{3,2},{4,3},{5,4},{6,5},{7,6},{8,7},{9,8},{10,9... | collective-permute-start | bytes 1544 | tf_op jit(solution)/shard_map/ppermute | solution.py:22
  284.1 10.0 %collective-permute-start.52 = (f32[4,2,16]{1,2,0:T(8,128)S(1)}, f32[4,2,16]{1,2,0:T(8,128)S(1)}, u32[]{:S(2)}, u32[]{:S(2)}) collective-permute-start(f32[4,2,16]{1,2,0:T(8,128)S(1)} %collective-permute-done.50), channel_id=1, source_target_pairs={{0,1},{1,2},{2,3},{3,4},{4,5},{5,6},{6,7},{7,8},{8,9},{9,10},{10,1... | collective-permute-start | bytes 1544 | tf_op jit(solution)/shard_map/ppermute | solution.py:19
  292.2 13.1 %collective-permute-start.53 = (f32[4,2,16]{1,2,0:T(8,128)S(1)}, f32[4,2,16]{1,2,0:T(8,128)S(1)}, u32[]{:S(2)}, u32[]{:S(2)}) collective-permute-start(f32[4,2,16]{1,2,0:T(8,128)S(1)} %collective-permute-done.51), channel_id=1, source_target_pairs={{0,15},{1,0},{2,1},{3,2},{4,3},{5,4},{6,5},{7,6},{8,7},{9,8},{10,9... | collective-permute-start | bytes 1544 | tf_op jit(solution)/shard_map/ppermute | solution.py:22
  294.1 13.1 %collective-permute-start.54 = (f32[4,2,16]{1,2,0:T(8,128)S(1)}, f32[4,2,16]{1,2,0:T(8,128)S(1)}, u32[]{:S(2)}, u32[]{:S(2)}) collective-permute-start(f32[4,2,16]{1,2,0:T(8,128)S(1)} %collective-permute-done.52), channel_id=1, source_target_pairs={{0,1},{1,2},{2,3},{3,4},{4,5},{5,6},{6,7},{7,8},{8,9},{9,10},{10,1... | collective-permute-start | bytes 1544 | tf_op jit(solution)/shard_map/ppermute | solution.py:19
  305.3 14.9 %collective-permute-start.55 = (f32[4,2,16]{1,2,0:T(8,128)S(1)}, f32[4,2,16]{1,2,0:T(8,128)S(1)}, u32[]{:S(2)}, u32[]{:S(2)}) collective-permute-start(f32[4,2,16]{1,2,0:T(8,128)S(1)} %collective-permute-done.53), channel_id=1, source_target_pairs={{0,15},{1,0},{2,1},{3,2},{4,3},{5,4},{6,5},{7,6},{8,7},{9,8},{10,9... | collective-permute-start | bytes 1544 | tf_op jit(solution)/shard_map/ppermute | solution.py:22
  307.2 13.7 %collective-permute-start.56 = (f32[4,2,16]{1,2,0:T(8,128)S(1)}, f32[4,2,16]{1,2,0:T(8,128)S(1)}, u32[]{:S(2)}, u32[]{:S(2)}) collective-permute-start(f32[4,2,16]{1,2,0:T(8,128)S(1)} %collective-permute-done.54), channel_id=1, source_target_pairs={{0,1},{1,2},{2,3},{3,4},{4,5},{5,6},{6,7},{7,8},{8,9},{9,10},{10,1... | collective-permute-start | bytes 1544 | tf_op jit(solution)/shard_map/ppermute | solution.py:19
  (107 other events, 2487.1 us)
